TPU v7x, 32 devices: a whole 2x2x4 slice. The times are simulated.
32 devices in a mesh: dp: 4 (over y, x), seq: 8 (over z, core).
Axes of the slice: x: 2, y: 2, z: 4, core: 2. Of those that a mesh axis runs over, the one named last changes fastest.
Arguments:
- asking_vectors_matrix: bfloat16 [4, 1024, 2048], P('dp', 'seq'), may hold values from -6 to 6
- matched_keys_matrix: bfloat16 [4, 1024, 2048], P('dp', 'seq'), may hold values from -6 to 6
- carried_vectors_matrix: bfloat16 [4, 1024, 2048], P('dp', 'seq'), may hold values from -6 to 6
- upstream_cotangent: bfloat16 [4, 1024, 2048], P('dp', 'seq'), may hold values from -6 to 6
- w_out: bfloat16 [2048, 2048], P('seq'), may hold values from -0.125 to 0.125
- panel_entry_offsets: int32 [4, 9], P('dp'), may hold values from 0 to 32, as said below
- rightward_panel_per_entry: int32 [4, 32], P('dp'), may hold values from 0 to 7, as said below
Outputs:
- layer_out: bfloat16 [4, 1024, 2048], P('dp', 'seq')
- q_grad: bfloat16 [4, 1024, 2048], P('dp', 'seq')
- k_grad: bfloat16 [4, 1024, 2048], P('dp', 'seq')
- v_grad: bfloat16 [4, 1024, 2048], P('dp', 'seq')
- w_out_grad: float32 [2048, 2048], P('seq')
Inputs may be any that keep to these rules, and one draw needn't show every extreme that they name: panel_entry_offsets[b, 0] is 0 and panel_entry_offsets never falls along a row; tile row r owns slots panel_entry_offsets[b, r] to panel_entry_offsets[b, r + 1] - 1, 1 to 8 of them, and its own tile r is among its blocks; in every subgraph one tile row holds all 8 tiles; panel_entry_offsets[b, 8], the used slots, lies between 16 and 32 and equals 32 for at least one subgraph. `rightward_panel_per_entry`: the slots of a tile row hold distinct column tiles in rising order; slots from panel_entry_offsets[b, 8] on hold arbitrary tile numbers that take no part.
All inputs are finite; a program needn't handle non-finite values.
Results may differ from a plain program's by a relative error of at most 0.034.
Values may be sent and summed in bfloat16 or wider, within the bound.
No kernel may reach another device: no remote copies, remote signals or barrier semaphores. Data moves between devices by JAX's collectives and lax.ppermute only.
A program may use at most 128 MiB of HBM per device.

v0:
```python
import math
import jax
import jax.numpy as jnp
from jax import lax
from jax.sharding import PartitionSpec as P

H = 16
HD = 128


def tile_mask(starts, columns, nodes):
    tile_count = starts.shape[0] - 1
    slot_count = columns.shape[0]
    tile_size = nodes // tile_count
    slot_index = jnp.arange(slot_count, dtype=jnp.int32)
    entry_row = jnp.sum((starts[1:][None, :] <= slot_index[:, None]).astype(jnp.int32), axis=1)
    tile_ids = jnp.arange(tile_count, dtype=jnp.int32)
    row_hot = (entry_row[:, None] == tile_ids[None, :]).astype(jnp.int32)
    col_hot = (columns[:, None] == tile_ids[None, :]).astype(jnp.int32)
    pairs = jnp.einsum("er,ec->rc", row_hot, col_hot) > 0
    full = jnp.broadcast_to(pairs[:, None, :, None], (tile_count, tile_size, tile_count, tile_size))
    return full.reshape(nodes, nodes)


def attend(q, k, v, g, allowed):
    factor = 1.0 / math.sqrt(q.shape[-1])
    scores = jnp.einsum("ihd,jhd->hij", q, k, preferred_element_type=jnp.float32) * factor
    masked = jnp.where(allowed[None], scores, -jnp.inf)
    row_max = jnp.max(masked, axis=2, keepdims=True)
    expd = jnp.where(allowed[None], jnp.exp(scores - row_max), 0.0)
    row_total = jnp.sum(expd, axis=2, keepdims=True)
    weighted = jnp.einsum(
        "hij,jhd->ihd", expd.astype(jnp.bfloat16), v, preferred_element_type=jnp.float32
    )
    totals = jnp.transpose(row_total[:, :, 0])[:, :, None]
    attended = (weighted / totals).astype(jnp.bfloat16)
    return (attended, expd, row_total)


def attend_back(q, k, v, g, attended, expd, row_total):
    factor = 1.0 / math.sqrt(q.shape[-1])
    prob = expd / row_total
    prob_low = prob.astype(jnp.bfloat16)
    v_grad = jnp.einsum("hij,ihd->jhd", prob_low, g, preferred_element_type=jnp.float32)
    prob_grad = jnp.einsum("ihd,jhd->hij", g, v, preferred_element_type=jnp.float32)
    delta = jnp.sum(attended.astype(jnp.float32) * g.astype(jnp.float32), axis=2)
    delta = jnp.transpose(delta)[:, :, None]
    score_grad = (prob * (prob_grad - delta) * factor).astype(jnp.bfloat16)
    q_grad = jnp.einsum("hij,jhd->ihd", score_grad, k, preferred_element_type=jnp.float32)
    k_grad = jnp.einsum("hij,ihd->jhd", score_grad, q, preferred_element_type=jnp.float32)
    return (q_grad.astype(jnp.bfloat16), k_grad.astype(jnp.bfloat16), v_grad.astype(jnp.bfloat16))


def shards(
    asking_vectors_matrix,
    matched_keys_matrix,
    carried_vectors_matrix,
    upstream_cotangent,
    w_out,
    panel_entry_offsets,
    rightward_panel_per_entry,
):
    nodes_here = asking_vectors_matrix.shape[1]
    width = asking_vectors_matrix.shape[2]
    n_seq = lax.axis_size("seq")
    nodes = nodes_here * n_seq
    grad_here = upstream_cotangent[0]
    grad_full = lax.all_gather(grad_here, "seq", axis=0, tiled=True)
    w_full = lax.all_gather(w_out, "seq", axis=0, tiled=True)
    stacked = jnp.stack(
        [asking_vectors_matrix[0], matched_keys_matrix[0], carried_vectors_matrix[0]]
    ).reshape(3, nodes_here, H, HD)
    heads = lax.all_to_all(stacked, "seq", split_axis=2, concat_axis=1, tiled=True)
    q_heads, k_heads, v_heads = (heads[0], heads[1], heads[2])
    local_heads = q_heads.shape[1]
    allowed = tile_mask(panel_entry_offsets[0], rightward_panel_per_entry[0], nodes)
    g_flat = lax.dot_general(
        grad_full, w_out, (((1,), (1,)), ((), ())), preferred_element_type=jnp.float32
    ).astype(jnp.bfloat16)
    g_heads = g_flat.reshape(nodes, local_heads, HD)
    attended, expd, row_total = attend(q_heads, k_heads, v_heads, g_heads, allowed)
    returned = lax.all_to_all(attended, "seq", split_axis=0, concat_axis=1, tiled=True)
    attended_nodes = returned.reshape(nodes_here, width)
    layer_out = jnp.dot(attended_nodes, w_full, preferred_element_type=jnp.float32)
    layer_out = layer_out.astype(jnp.bfloat16)[None]
    att_blocks = attended.reshape(n_seq, nodes_here, local_heads * HD)
    grad_blocks = grad_full.reshape(n_seq, nodes_here, width)
    terms = jnp.einsum(
        "bnf,bnk->bfk", att_blocks, grad_blocks, preferred_element_type=jnp.float32
    ).astype(jnp.bfloat16)
    w_rows = jnp.sum(terms.astype(jnp.float32), axis=0)
    batch = asking_vectors_matrix.shape[0] * lax.axis_size("dp")
    w_out_grad = lax.psum(w_rows, "dp") / batch
    q_g, k_g, v_g = attend_back(q_heads, k_heads, v_heads, g_heads, attended, expd, row_total)
    grads = jnp.stack([q_g, k_g, v_g])
    back = lax.all_to_all(grads, "seq", split_axis=1, concat_axis=2, tiled=True)
    back = back.reshape(3, 1, nodes_here, width)
    return (layer_out, back[0], back[1], back[2], w_out_grad)


def solution(mesh):
    return jax.shard_map(
        shards,
        mesh=mesh,
        in_specs=(
            P("dp", "seq", None),
            P("dp", "seq", None),
            P("dp", "seq", None),
            P("dp", "seq", None),
            P("seq", None),
            P("dp", None),
            P("dp", None),
        ),
        out_specs=(
            P("dp", "seq", None),
            P("dp", "seq", None),
            P("dp", "seq", None),
            P("dp", "seq", None),
            P("seq", None),
        ),
        check_vma=False,
    )
```

profile of v0, /device:TPU:0, one launch (start us, length us, event | category | flops | bytes accessed | tf_op | source)
XLA Modules:
  0.0 276.4 jit_solution(7157705828374576800)
XLA Ops:
  7.2 0.0 all-gather.6.cloned.1.call-start
  7.2 0.7 all-gather.6.cloned.1.call-update
  7.9 1.3 copy.117
  9.2 1.3 copy.118
  10.5 1.3 copy.119
  11.9 0.0 copy-start.4
  11.9 0.0 copy-start.5
  11.9 0.2 pad_maximum_fusion
  12.1 1.2 copy.120
  13.3 6.3 %all-to-all-start = ((bf16[3,128,16,128]{1,3,0,2:T(8,128)(2,1)}), bf16[3,128,16,128]{1,3,0,2:T(8,128)(2,1)S(1)}, u32[]{:S(2)}, u32[]{:S(2)}) async-start(bf16[3,128,16,128]{1,3,0,2:T(8,128)(2,1)} %copy.120), calls=%async_computation | async-start | bytes 3145728 | tf_op jit(solution)/shard_map/all_to_all | solution.py:73
  19.6 0.0 all-reduce.2.cloned.1.call-start
  19.7 0.0 copy-done.4
  19.7 0.1 slice_bitcast_fusion
  19.8 0.1 convert_reduce_fusion.1
  19.9 0.0 copy-done.5
  19.9 0.3 convolution_compare_fusion
  20.1 0.1 copy.123
  20.2 0.3 broadcast_in_dim.38
  20.5 1.5 copy.157
  22.0 69.1 %all-to-all-done = bf16[3,128,16,128]{1,3,0,2:T(8,128)(2,1)S(1)} async-done(((bf16[3,128,16,128]{1,3,0,2:T(8,128)(2,1)}), bf16[3,128,16,128]{1,3,0,2:T(8,128)(2,1)S(1)}, u32[]{:S(2)}, u32[]{:S(2)}) %all-to-all-start) | async-done | bytes 1572896 | tf_op jit(solution)/shard_map/all_to_all | solution.py:73
  91.2 0.9 copy.121
  92.1 0.1 fusion.43
  92.3 0.3 copy.122
  92.6 0.2 squeeze.22
  92.9 0.0 copy-start
  92.9 7.1 %fusion.44 = (f32[2,1024]{1,0:T(2,128)S(1)}, f32[2,1024,1024]{1,2,0:T(8,128)}) fusion(pred[1024,1024]{0,1:T(8,128)(4,1)} %bitcast.89, bf16[1024,2,128]{2,0,1:T(8,128)(2,1)S(1)} %bitcast.86, bf16[1024,2,128]{2,0,1:T(8,128)(2,1)S(1)} %bitcast.82), kind=kOutput, calls=%fused_computation.48 | convolution fusion | flops 1086325760 | bytes 10493952 | tf_op jit(solution)/shard_map/sub | solution.py:30
  100.0 0.0 all-gather.6.cloned.1.call-done
  100.0 0.0 copy-done
  100.0 3.5 %fusion.27 = bf16[1024,256]{0,1:T(8,128)(2,1)S(1)} fusion(bf16[256,2048]{1,0:T(8,128)(2,1)S(1)} %copy-done, bf16[1,1024,2048]{2,1,0:T(8,128)(2,1)} %all-gather.6.cloned.1.call-done), kind=kOutput, calls=%fused_computation.28 | convolution fusion | flops 1074003968 | bytes 5767168 | tf_op jit(solution)/shard_map/dot_general | solution.py:77
  103.5 0.0 copy-start.1
  103.5 0.0 copy-start.3
  103.5 4.5 %multiply_reduce_fusion = (f32[1024,2]{0,1:T(2,128)S(1)}, bf16[1024,2,128]{0,2,1:T(8,128)(2,1)S(1)}) fusion(bf16[1024,256]{0,1:T(8,128)(2,1)S(1)} %fusion.27, f32[1024,2]{0,1:T(2,128)S(1)} %bitcast.93, bf16[1024,2,128]{0,2,1:T(8,128)(2,1)S(1)} %squeeze.22, f32[2,1024,1024]{1,2,0:T(8,128)} %get-tuple-element.12), kind=kOutput, calls=%fused_computation.34 | convolution fusion | flops 540538880 | bytes 9977856 | tf_op jit(solution)/shard_map/hij,jhd->ihd/dot_general | solution.py:32
  108.0 0.0 copy-done.1
  108.0 0.1 copy.153
  108.1 0.2 copy-done.3
  108.3 3.6 %convert_reduce_fusion = f32[256,2048]{1,0:T(8,128)} fusion(bf16[8,128,2048]{2,1,0:T(8,128)(2,1)S(1)} %bitcast.95, bf16[8,128,256]{1,0,2:T(8,128)(2,1)S(1)} %bitcast.92), kind=kOutput, calls=%fused_computation.1 | convolution fusion | flops 1085800448 | bytes 6815744 | tf_op jit(solution)/shard_map/bnf,bnk->bfk/dot_general | solution.py:88
  111.9 0.0 all-reduce.2.cloned.1.call-update
  111.9 0.0 all-gather.4.cloned.1.call-start
  112.0 0.7 all-gather.4.cloned.1.call-update
  112.7 1.1 copy.127
  113.8 3.7 %all-to-all-start.1 = ((bf16[1024,2,128]{2,1,0:T(2,128)(2,1)}), bf16[1024,2,128]{2,1,0:T(2,128)(2,1)S(1)}, u32[]{:S(2)}, u32[]{:S(2)}) async-start(bf16[1024,2,128]{2,1,0:T(2,128)(2,1)} %copy.127), calls=%async_computation.1 | async-start | bytes 1048576 | tf_op jit(solution)/shard_map/all_to_all | solution.py:82
  117.5 0.0 copy-done.2
  117.5 4.3 %multiply_convert_fusion = bf16[2,1024,1024]{1,2,0:T(8,128)(2,1)S(1)} fusion(f32[2,1024]{1,0:T(2,128)S(1)} %bitcast.94, f32[2,1024,1024]{1,2,0:T(8,128)} %get-tuple-element.12, f32[2,1024]{1,0:T(2,128)S(1)} %get-tuple-element.11, bf16[1024,2,128]{0,2,1:T(8,128)(2,1)S(1)} %bitcast.90, bf16[1024,2,128]{0,2,1:T(8,128)(2,1)S(1)} %squeeze.22), kind=kOutput, calls=%fused_computation.2 | convolution fusion | flops 547356672 | bytes 13647872 | tf_op jit(solution)/shard_map/ihd,jhd->hij/dot_general | solution.py:45
  121.8 0.8 fusion.30
  122.6 1.6 fusion.31
  124.2 5.0 %fusion.32 = bf16[1,1024,2,128]{1,3,2,0:T(8,128)(2,1)S(1)} fusion(bf16[1024,2,128]{0,2,1:T(8,128)(2,1)S(1)} %bitcast.91, f32[2,1024,1024]{1,2,0:T(8,128)} %get-tuple-element.12, f32[2,1024]{1,0:T(2,128)S(1)} %get-tuple-element.11), kind=kOutput, calls=%fused_computation.31 | convolution fusion | flops 541327360 | bytes 9445376 | tf_op jit(solution)/shard_map/hij,ihd->jhd/dot_general | solution.py:44
  129.2 0.2 pad_maximum_fusion.1
  129.4 3.0 %copy.138 = bf16[3,1024,2,128]{3,2,0,1:T(2,128)(2,1)} copy(bf16[3,1024,2,128]{1,3,2,0:T(8,128)(2,1)S(1)} %pad_maximum_fusion.1) | data formatting | bytes 3145728 | tf_op jit(solution)/shard_map/stack | solution.py:95
  132.4 0.2 all-to-all-done.1
  132.6 4.6 %all-to-all-start.2 = ((bf16[3,1024,2,128]{3,2,0,1:T(2,128)(2,1)}), bf16[3,1024,2,128]{3,2,0,1:T(2,128)(2,1)S(1)}, u32[]{:S(2)}, u32[]{:S(2)}) async-start(bf16[3,1024,2,128]{3,2,0,1:T(2,128)(2,1)} %copy.138), calls=%async_computation.2 | async-start | bytes 3145728 | tf_op jit(solution)/shard_map/all_to_all | solution.py:96
  137.2 0.1 copy.128
  137.3 0.3 copy.129
  137.6 43.1 %all-reduce.2.cloned.1.call-done = f32[256,2048]{1,0:T(8,128)} async-done(((f32[256,2048]{1,0:T(8,128)}), f32[256,2048]{1,0:T(8,128)}) %all-reduce.2.cloned.1.call-update) | async-done | bytes 2097168 | tf_op jit(solution)/shard_map/psum | solution.py:93
  180.7 3.1 %broadcast_multiply_fusion = f32[256,2048]{1,0:T(8,128)} fusion(f32[256,2048]{1,0:T(8,128)} %all-reduce.2.cloned.1.call-done), kind=kLoop, calls=%fused_computation.33 | loop fusion | flops 524288 | bytes 4194304 | tf_op jit(solution)/shard_map/div | solution.py:93
  183.8 0.0 all-to-all-done.2
  183.8 1.2 fusion.42
  185.0 0.4 copy.139
  185.4 1.2 squeeze.26
  186.6 0.4 copy.140
  186.9 1.2 squeeze.27
  188.1 0.4 copy.141
  188.5 1.2 squeeze.28
  189.7 74.8 %all-gather.4.cloned.1.call-done = bf16[2048,2048]{1,0:T(8,128)(2,1)} async-done(((bf16[256,2048]{1,0:T(8,128)(2,1)}), bf16[2048,2048]{1,0:T(8,128)(2,1)}) %all-gather.4.cloned.1.call-update) | async-done | bytes 8388624 | tf_op jit(solution)/shard_map/all_gather | solution.py:69
  264.5 5.5 %fusion.14 = bf16[1,128,2048]{2,1,0:T(8,128)(2,1)} fusion(bf16[128,2048]{0,1:T(8,128)(2,1)S(1)} %bitcast.84, bf16[2048,2048]{1,0:T(8,128)(2,1)} %all-gather.4.cloned.1.call-done), kind=kOutput, calls=%fused_computation.19 | convolution fusion | flops 1074003968 | bytes 9437184 | tf_op jit(solution)/shard_map/dot_general | solution.py:84
  (3 shorter events, 0.1 us)
Async XLA Ops:
  7.2 92.9 %all-gather.6.cloned.1.call-start = ((), (), s32[]{:S(2)}) async-start(), calls=%async_computation.5 | async-start | bytes 4718592 | tf_op jit(solution)/shard_map/all_gather | solution.py:68
  11.9 7.8 %copy-start.4 = (s32[1,9]{1,0:T(1,128)S(1)}, s32[1,9]{1,0:T(1,128)}, u32[]{:S(2)}) copy-start(s32[1,9]{1,0:T(1,128)} %param.12) | copy-start | bytes 112
  11.9 8.0 %copy-start.5 = (s32[1,32]{1,0:T(1,128)S(1)}, s32[1,32]{1,0:T(1,128)}, u32[]{:S(2)}) copy-start(s32[1,32]{1,0:T(1,128)} %param.13) | copy-start | bytes 388
  13.3 77.9 %all-to-all-start = ((bf16[3,128,16,128]{1,3,0,2:T(8,128)(2,1)}), bf16[3,128,16,128]{1,3,0,2:T(8,128)(2,1)S(1)}, u32[]{:S(2)}, u32[]{:S(2)}) async-start(bf16[3,128,16,128]{1,3,0,2:T(8,128)(2,1)} %copy.120), calls=%async_computation | async-start | bytes 3145728 | tf_op jit(solution)/shard_map/all_to_all | solution.py:73
  19.6 161.0 %all-reduce.2.cloned.1.call-start = ((), (), s32[]{:S(2)}) async-start(), calls=%async_computation.4 | async-start | bytes 4194304 | tf_op jit(solution)/shard_map/psum | solution.py:93
  92.9 7.2 %copy-start = (bf16[256,2048]{1,0:T(8,128)(2,1)S(1)}, bf16[256,2048]{1,0:T(8,128)(2,1)}, u32[]{:S(2)}) copy-start(bf16[256,2048]{1,0:T(8,128)(2,1)} %param.11) | copy-start | bytes 3145732
  103.5 4.5 %copy-start.1 = (bf16[1024,256]{0,1:T(8,128)(2,1)}, bf16[1024,256]{0,1:T(8,128)(2,1)S(1)}, u32[]{:S(2)}) copy-start(bf16[1024,256]{0,1:T(8,128)(2,1)S(1)} %fusion.27) | copy-start | bytes 1572868
  103.5 4.8 %copy-start.3 = (bf16[1,1024,2048]{2,1,0:T(8,128)(2,1)S(1)}, bf16[1,1024,2048]{2,1,0:T(8,128)(2,1)}, u32[]{:S(2)}) copy-start(bf16[1,1024,2048]{2,1,0:T(8,128)(2,1)} %all-gather.6.cloned.1.call-done) | copy-start | bytes 12582916
  111.9 5.6 %copy-start.2 = (bf16[1024,256]{0,1:T(8,128)(2,1)S(1)}, bf16[1024,256]{0,1:T(8,128)(2,1)}, u32[]{:S(2)}) copy-start(bf16[1024,256]{0,1:T(8,128)(2,1)} %copy-done.1) | copy-start | bytes 1572868
  111.9 152.5 %all-gather.4.cloned.1.call-start = ((), (), s32[]{:S(2)}) async-start(), calls=%async_computation.3 | async-start | bytes 9437184 | tf_op jit(solution)/shard_map/all_gather | solution.py:69
  113.8 18.8 %all-to-all-start.1 = ((bf16[1024,2,128]{2,1,0:T(2,128)(2,1)}), bf16[1024,2,128]{2,1,0:T(2,128)(2,1)S(1)}, u32[]{:S(2)}, u32[]{:S(2)}) async-start(bf16[1024,2,128]{2,1,0:T(2,128)(2,1)} %copy.127), calls=%async_computation.1 | async-start | bytes 1048576 | tf_op jit(solution)/shard_map/all_to_all | solution.py:82
  132.6 51.2 %all-to-all-start.2 = ((bf16[3,1024,2,128]{3,2,0,1:T(2,128)(2,1)}), bf16[3,1024,2,128]{3,2,0,1:T(2,128)(2,1)S(1)}, u32[]{:S(2)}, u32[]{:S(2)}) async-start(bf16[3,1024,2,128]{3,2,0,1:T(2,128)(2,1)} %copy.138), calls=%async_computation.2 | async-start | bytes 3145728 | tf_op jit(solution)/shard_map/all_to_all | solution.py:96
Sparse Core Ops, SparseCore 0:
  9.6 83.0 all-gather.5
  112.1 68.5 all-reduce.1
  182.4 82.0 all-gather.3
where the time goes:
time: 277 us; the launch traced here: 276 us
  waiting for transfers between devices  189 us (68%)
  matrix products  36.1 us (13%)
  local copies, waits for them, and re-layouts  19.5 us (7%)
  starting transfers between devices  14.8 us (5%)
  between operations  14 us (5%)
  other arithmetic  3.58 us (1%)
    all_gather x1, waiting for transfers between devices, shards(): w_full = lax.all_gather(w_out, 'seq', axis=0, tiled=True)  74.8 us
    all_to_all x1, waiting for transfers between devices, shards(): lax.all_to_all(stacked, 'seq', split_axis=2, concat_axis=1, tiled=True)  69.1 us
    psum x1, waiting for transfers between devices, shards(): w_out_grad = lax.psum(w_rows, 'dp') / batch  43.1 us
    sub x1, matrix products, attend(): expd = jnp.where(allowed[None], jnp.exp(scores - row_max), 0.0)  7.15 us
    all_to_all x1, starting transfers between devices, shards(): lax.all_to_all(stacked, 'seq', split_axis=2, concat_axis=1, tiled=True)  6.33 us
    unnamed x17, local copies, waits for them, and re-layouts  5.75 us
  transfers between devices with their start and end apart: 6, of which 4 were waited for; matrix products, arithmetic and copies ran while one was open for 15% of the time, Pallas kernels for 0%

commit v1 on v0

--- a/solution.py
+++ b/solution.py
@@ -6,6 +6,29 @@
 
 H = 16
 HD = 128
+
+
+def split_up(value, dim, length):
+    lengths = value.shape
+    parts = value.reshape(*lengths[:dim], length, lengths[dim] // length, *lengths[dim + 1 :])
+    return jnp.moveaxis(parts, dim, 0)
+
+
+def in_order(blocks, dim):
+    shape = list(blocks.shape[1:])
+    shape[dim] *= blocks.shape[0]
+    return jnp.moveaxis(blocks, 0, dim).reshape(shape)
+
+
+def exchange_in_pairs(x, axis, split_dim, concat_dim):
+    size, index = (lax.axis_size(axis), lax.axis_index(axis))
+    parts = split_up(x, split_dim, size)
+    outs = [parts[index]]
+    for step in range(1, size):
+        sent = parts[index ^ step]
+        outs.append(lax.ppermute(sent, axis, [(i, i ^ step) for i in range(size)]))
+    parts = jnp.stack(outs)[index ^ jnp.arange(size)]
+    return in_order(parts, concat_dim)
 
 
 def tile_mask(starts, columns, nodes):
@@ -70,7 +93,7 @@
     stacked = jnp.stack(
         [asking_vectors_matrix[0], matched_keys_matrix[0], carried_vectors_matrix[0]]
     ).reshape(3, nodes_here, H, HD)
-    heads = lax.all_to_all(stacked, "seq", split_axis=2, concat_axis=1, tiled=True)
+    heads = exchange_in_pairs(stacked, "seq", 2, 1)
     q_heads, k_heads, v_heads = (heads[0], heads[1], heads[2])
     local_heads = q_heads.shape[1]
     allowed = tile_mask(panel_entry_offsets[0], rightward_panel_per_entry[0], nodes)

time: 277 us -> 275 us (level)
  waiting for transfers between devices: 189 us -> 174 us
  starting transfers between devices: 14.8 us -> 24.9 us
    all_to_all x1 -> x0, waiting for transfers between devices: 69.1 us -> none  [shards(): lax.all_to_all(stacked, 'seq', split_axis=2, concat_axis=1, tiled=True)]
    ppermute x0 -> x7, waiting for transfers between devices: none -> 38.7 us  [exchange_in_pairs(): outs.append(lax.ppermute(sent, axis, [(i, i ^ step) for i in range(size)]))]
    all_gather x1, waiting for transfers between devices: 0.01 us -> 15.3 us  [shards(): grad_full = lax.all_gather(grad_here, 'seq', axis=0, tiled=True)]
    ppermute x0 -> x7, starting transfers between devices: none -> 9.69 us  [exchange_in_pairs(): outs.append(lax.ppermute(sent, axis, [(i, i ^ step) for i in range(size)]))]
    all_to_all x1, starting transfers between devices: 3.71 us -> 10.4 us  [shards(): lax.all_to_all(attended, 'seq', split_axis=0, concat_axis=1, tiled=True)]
    all_to_all x1 -> x0, starting transfers between devices: 6.33 us -> none  [shards(): lax.all_to_all(stacked, 'seq', split_axis=2, concat_axis=1, tiled=True)]
    unnamed x17 -> x28, local copies, waits for them, and re-layouts: 5.75 us -> 4.47 us
  transfers between devices with their start and end apart: 6 -> 12, of which waited for: 4 -> 9; matrix products, arithmetic and copies ran while one was open for 15% -> 16% of each run, Pallas kernels for 0% -> 0%
where the time goes in v1:
time: 275 us; the launch traced here: 274 us
  waiting for transfers between devices  174 us (63%)
  matrix products  36.1 us (13%)
  starting transfers between devices  24.9 us (9%)
  local copies, waits for them, and re-layouts  19.5 us (7%)
  between operations  14.1 us (5%)
  other arithmetic  4.95 us (2%)
    all_gather x1, waiting for transfers between devices, shards(): w_full = lax.all_gather(w_out, 'seq', axis=0, tiled=True)  74.8 us
    psum x1, waiting for transfers between devices, shards(): w_out_grad = lax.psum(w_rows, 'dp') / batch  43.9 us
    ppermute x7, waiting for transfers between devices, exchange_in_pairs(): outs.append(lax.ppermute(sent, axis, [(i, i ^ step) for i in range(size)]))  38.7 us
    all_gather x1, waiting for transfers between devices, shards(): grad_full = lax.all_gather(grad_here, 'seq', axis=0, tiled=True)  15.3 us
    all_to_all x1, starting transfers between devices, shards(): lax.all_to_all(attended, 'seq', split_axis=0, concat_axis=1, tiled=True)  10.4 us
    ppermute x7, starting transfers between devices, exchange_in_pairs(): outs.append(lax.ppermute(sent, axis, [(i, i ^ step) for i in range(size)]))  9.69 us
    sub x1, matrix products, attend(): expd = jnp.where(allowed[None], jnp.exp(scores - row_max), 0.0)  7.13 us
  transfers between devices with their start and end apart: 12, of which 9 were waited for; matrix products, arithmetic and copies ran while one was open for 16% of the time, Pallas kernels for 0%

profile of v1, /device:TPU:0, one launch (start us, length us, event | category | flops | bytes accessed | tf_op | source)
XLA Modules:
  0.0 274.1 jit_solution(10986695980167896737)
XLA Ops:
  7.2 0.0 all-gather.6.cloned.1.call-start
  7.2 0.7 all-gather.6.cloned.1.call-update
  7.9 0.0 all-reduce.2.cloned.1.call-start
  8.0 1.5 pad_maximum_fusion
  9.5 1.1 reshape_reshape.3
  10.7 1.4 constant_dynamic-slice_fusion
  12.1 0.7 copy.177
  12.8 0.5 collective-permute-start
  13.3 0.7 copy.176
  14.0 2.6 collective-permute-start.1
  16.6 0.2 collective-permute-start.2
  16.8 2.8 %collective-permute-start.3 = (bf16[3,128,2,128]{3,1,2,0:T(8,128)(2,1)S(1)}, bf16[3,128,2,128]{3,1,2,0:T(8,128)(2,1)S(1)}, u32[]{:S(2)}, u32[]{:S(2)}) collective-permute-start(bf16[3,128,2,128]{3,1,2,0:T(8,128)(2,1)S(1)} %bitcast.133), channel_id=1, source_target_pairs={{0,4},{1,5},{2,6},{3,7},{4,0},{5,1},{6,2},{7,3},{8,12},{9,13},{10,... | collective-permute-start | bytes 589832 | tf_op jit(solution)/shard_map/ppermute | solution.py:29
  19.6 0.1 collective-permute-start.4
  19.8 0.1 slice_bitcast_fusion
  19.9 0.1 convert_reduce_fusion.1
  20.0 0.3 convolution_compare_fusion
  20.2 0.1 copy.118
  20.3 0.3 broadcast_in_dim.39
  20.7 1.5 copy.170
  22.2 3.6 %collective-permute-start.5 = (bf16[3,128,2,128]{3,1,2,0:T(8,128)(2,1)S(1)}, bf16[3,128,2,128]{3,1,2,0:T(8,128)(2,1)S(1)}, u32[]{:S(2)}, u32[]{:S(2)}) collective-permute-start(bf16[3,128,2,128]{3,1,2,0:T(8,128)(2,1)S(1)} %bitcast.131), channel_id=1, source_target_pairs={{0,6},{1,7},{2,4},{3,5},{4,2},{5,3},{6,0},{7,1},{8,14},{9,15},{10,... | collective-permute-start | bytes 589832 | tf_op jit(solution)/shard_map/ppermute | solution.py:29
  25.8 1.0 bitcast_dynamic-update-slice_fusion.6
  26.8 6.9 %collective-permute-done.1 = bf16[3,128,2,128]{3,1,2,0:T(8,128)(2,1)S(1)} collective-permute-done((bf16[3,128,2,128]{3,1,2,0:T(8,128)(2,1)}, bf16[3,128,2,128]{3,1,2,0:T(8,128)(2,1)S(1)}, u32[]{:S(2)}, u32[]{:S(2)}) %collective-permute-start.1) | collective-permute-done | bytes 196640 | tf_op jit(solution)/shard_map/ppermute | solution.py:29
  33.7 10.2 %collective-permute-done.2 = bf16[3,128,2,128]{3,1,2,0:T(8,128)(2,1)S(1)} collective-permute-done((bf16[3,128,2,128]{3,1,2,0:T(8,128)(2,1)S(1)}, bf16[3,128,2,128]{3,1,2,0:T(8,128)(2,1)S(1)}, u32[]{:S(2)}, u32[]{:S(2)}) %collective-permute-start.2) | collective-permute-done | bytes 196640 | tf_op jit(solution)/shard_map/ppermute | solution.py:29
  44.0 4.5 %collective-permute-done.4 = bf16[3,128,2,128]{3,1,2,0:T(8,128)(2,1)S(1)} collective-permute-done((bf16[3,128,2,128]{3,1,2,0:T(8,128)(2,1)S(1)}, bf16[3,128,2,128]{3,1,2,0:T(8,128)(2,1)S(1)}, u32[]{:S(2)}, u32[]{:S(2)}) %collective-permute-start.4) | collective-permute-done | bytes 196640 | tf_op jit(solution)/shard_map/ppermute | solution.py:29
  48.5 10.3 %collective-permute-done.5 = bf16[3,128,2,128]{3,1,2,0:T(8,128)(2,1)S(1)} collective-permute-done((bf16[3,128,2,128]{3,1,2,0:T(8,128)(2,1)S(1)}, bf16[3,128,2,128]{3,1,2,0:T(8,128)(2,1)S(1)}, u32[]{:S(2)}, u32[]{:S(2)}) %collective-permute-start.5) | collective-permute-done | bytes 196640 | tf_op jit(solution)/shard_map/ppermute | solution.py:29
  58.8 6.9 %collective-permute-done.6 = bf16[3,128,2,128]{3,1,2,0:T(8,128)(2,1)S(1)} collective-permute-done((bf16[3,128,2,128]{3,1,2,0:T(8,128)(2,1)S(1)}, bf16[3,128,2,128]{3,1,2,0:T(8,128)(2,1)S(1)}, u32[]{:S(2)}, u32[]{:S(2)}) %collective-permute-start.6) | collective-permute-done | bytes 196640 | tf_op jit(solution)/shard_map/ppermute | solution.py:29
  65.7 0.9 gather_fusion
  66.6 0.1 fusion.45
  66.8 0.3 copy.117
  67.1 0.2 squeeze.50
  67.4 0.0 copy-start
  67.4 7.1 %fusion.46 = (f32[2,1024]{1,0:T(2,128)S(1)}, f32[2,1024,1024]{1,2,0:T(8,128)}) fusion(pred[1024,1024]{0,1:T(8,128)(4,1)} %bitcast.126, bf16[1024,2,128]{2,0,1:T(8,128)(2,1)S(1)} %bitcast.123, bf16[1024,2,128]{2,0,1:T(8,128)(2,1)S(1)} %bitcast.119), kind=kOutput, calls=%fused_computation.76 | convolution fusion | flops 1086325760 | bytes 10493952 | tf_op jit(solution)/shard_map/sub | solution.py:53
  74.5 15.3 %all-gather.6.cloned.1.call-done = bf16[1,1024,2048]{2,1,0:T(8,128)(2,1)} async-done(((bf16[1,128,2048]{2,1,0:T(8,128)(2,1)}), bf16[1,1024,2048]{2,1,0:T(8,128)(2,1)}) %all-gather.6.cloned.1.call-update) | async-done | bytes 4194320 | tf_op jit(solution)/shard_map/all_gather | solution.py:91
  89.8 3.5 %fusion.27 = bf16[1024,256]{0,1:T(8,128)(2,1)S(1)} fusion(bf16[256,2048]{1,0:T(8,128)(2,1)S(1)} %copy-done, bf16[1,1024,2048]{2,1,0:T(8,128)(2,1)} %all-gather.6.cloned.1.call-done), kind=kOutput, calls=%fused_computation.29 | convolution fusion | flops 1074003968 | bytes 5767168 | tf_op jit(solution)/shard_map/dot_general | solution.py:100
  93.3 4.5 %multiply_reduce_fusion = (f32[1024,2]{0,1:T(2,128)S(1)}, bf16[1024,2,128]{0,2,1:T(8,128)(2,1)S(1)}) fusion(bf16[1024,256]{0,1:T(8,128)(2,1)S(1)} %fusion.27, f32[1024,2]{0,1:T(2,128)S(1)} %bitcast.135, bf16[1024,2,128]{0,2,1:T(8,128)(2,1)S(1)} %squeeze.50, f32[2,1024,1024]{1,2,0:T(8,128)} %get-tuple-element.20), kind=kOutput, calls=%fused_computation.35 | convolution fusion | flops 540538880 | bytes 9977856 | tf_op jit(solution)/shard_map/hij,jhd->ihd/dot_general | solution.py:55
  97.8 0.1 copy.156
  97.9 0.2 copy-done.3
  98.0 3.6 %convert_reduce_fusion = f32[256,2048]{1,0:T(8,128)} fusion(bf16[8,128,2048]{2,1,0:T(8,128)(2,1)S(1)} %bitcast.137, bf16[8,128,256]{1,0,2:T(8,128)(2,1)S(1)} %bitcast.129), kind=kOutput, calls=%fused_computation.2 | convolution fusion | flops 1085800448 | bytes 6815744 | tf_op jit(solution)/shard_map/bnf,bnk->bfk/dot_general | solution.py:111
  101.7 0.0 all-reduce.2.cloned.1.call-update
  101.7 0.0 all-gather.4.cloned.1.call-start
  101.7 0.7 all-gather.4.cloned.1.call-update
  102.4 1.1 copy.122
  103.5 10.4 %all-to-all-start = ((bf16[1024,2,128]{2,1,0:T(2,128)(2,1)}), bf16[1024,2,128]{2,1,0:T(2,128)(2,1)S(1)}, u32[]{:S(2)}, u32[]{:S(2)}) async-start(bf16[1024,2,128]{2,1,0:T(2,128)(2,1)} %copy.122), calls=%async_computation | async-start | bytes 1048576 | tf_op jit(solution)/shard_map/all_to_all | solution.py:105
  114.0 4.4 %multiply_convert_fusion = bf16[2,1024,1024]{1,2,0:T(8,128)(2,1)S(1)} fusion(f32[2,1024]{1,0:T(2,128)S(1)} %bitcast.136, f32[2,1024,1024]{1,2,0:T(8,128)} %get-tuple-element.20, f32[2,1024]{1,0:T(2,128)S(1)} %get-tuple-element.19, bf16[1024,2,128]{0,2,1:T(8,128)(2,1)S(1)} %bitcast.127, bf16[1024,2,128]{0,2,1:T(8,128)(2,1)S(1)} %squeeze.50), kind=kOutput, calls=%fused_computation.3 | convolution fusion | flops 547356672 | bytes 13647872 | tf_op jit(solution)/shard_map/ihd,jhd->hij/dot_general | solution.py:68
  118.4 0.8 fusion.30
  119.2 1.5 fusion.31
  120.7 5.0 %fusion.32 = bf16[1,1024,2,128]{1,3,2,0:T(8,128)(2,1)S(1)} fusion(bf16[1024,2,128]{0,2,1:T(8,128)(2,1)S(1)} %bitcast.128, f32[2,1024,1024]{1,2,0:T(8,128)} %get-tuple-element.20, f32[2,1024]{1,0:T(2,128)S(1)} %get-tuple-element.19), kind=kOutput, calls=%fused_computation.32 | convolution fusion | flops 541327360 | bytes 9445376 | tf_op jit(solution)/shard_map/hij,ihd->jhd/dot_general | solution.py:67
  125.7 0.2 pad_maximum_fusion.1
  125.9 3.1 %copy.133 = bf16[3,1024,2,128]{3,2,0,1:T(2,128)(2,1)} copy(bf16[3,1024,2,128]{1,3,2,0:T(8,128)(2,1)S(1)} %pad_maximum_fusion.1) | data formatting | bytes 3145728 | tf_op jit(solution)/shard_map/stack | solution.py:118
  129.0 0.4 all-to-all-done
  129.3 4.7 %all-to-all-start.1 = ((bf16[3,1024,2,128]{3,2,0,1:T(2,128)(2,1)}), bf16[3,1024,2,128]{3,2,0,1:T(2,128)(2,1)S(1)}, u32[]{:S(2)}, u32[]{:S(2)}) async-start(bf16[3,1024,2,128]{3,2,0,1:T(2,128)(2,1)} %copy.133), calls=%async_computation.1 | async-start | bytes 3145728 | tf_op jit(solution)/shard_map/all_to_all | solution.py:119
  134.0 0.1 copy.123
  134.1 0.3 copy.124
  134.4 43.9 %all-reduce.2.cloned.1.call-done = f32[256,2048]{1,0:T(8,128)} async-done(((f32[256,2048]{1,0:T(8,128)}), f32[256,2048]{1,0:T(8,128)}) %all-reduce.2.cloned.1.call-update) | async-done | bytes 2097168 | tf_op jit(solution)/shard_map/psum | solution.py:116
  178.3 3.1 %broadcast_multiply_fusion = f32[256,2048]{1,0:T(8,128)} fusion(f32[256,2048]{1,0:T(8,128)} %all-reduce.2.cloned.1.call-done), kind=kLoop, calls=%fused_computation.34 | loop fusion | flops 524288 | bytes 4194304 | tf_op jit(solution)/shard_map/div | solution.py:116
  181.4 1.2 fusion.44
  182.7 0.4 copy.134
  183.0 1.2 squeeze.54
  184.2 0.4 copy.135
  184.6 1.2 squeeze.55
  185.8 0.4 copy.136
  186.1 1.2 squeeze.56
  187.3 74.8 %all-gather.4.cloned.1.call-done = bf16[2048,2048]{1,0:T(8,128)(2,1)} async-done(((bf16[256,2048]{1,0:T(8,128)(2,1)}), bf16[2048,2048]{1,0:T(8,128)(2,1)}) %all-gather.4.cloned.1.call-update) | async-done | bytes 8388624 | tf_op jit(solution)/shard_map/all_gather | solution.py:92
  262.1 5.5 %fusion.14 = bf16[1,128,2048]{2,1,0:T(8,128)(2,1)} fusion(bf16[128,2048]{0,1:T(8,128)(2,1)S(1)} %bitcast.121, bf16[2048,2048]{1,0:T(8,128)(2,1)} %all-gather.4.cloned.1.call-done), kind=kOutput, calls=%fused_computation.20 | convolution fusion | flops 1074003968 | bytes 9437184 | tf_op jit(solution)/shard_map/dot_general | solution.py:107
  (30 shorter events, 0.5 us)
Async XLA Ops:
  7.2 82.6 %all-gather.6.cloned.1.call-start = ((), (), s32[]{:S(2)}) async-start(), calls=%async_computation.4 | async-start | bytes 4718592 | tf_op jit(solution)/shard_map/all_gather | solution.py:91
  7.9 170.4 %all-reduce.2.cloned.1.call-start = ((), (), s32[]{:S(2)}) async-start(), calls=%async_computation.3 | async-start | bytes 4194304 | tf_op jit(solution)/shard_map/psum | solution.py:116
  9.5 10.3 %copy-start.4 = (s32[1,9]{1,0:T(1,128)S(1)}, s32[1,9]{1,0:T(1,128)}, u32[]{:S(2)}) copy-start(s32[1,9]{1,0:T(1,128)} %param.12) | copy-start | bytes 112
  9.5 10.4 %copy-start.5 = (s32[1,32]{1,0:T(1,128)S(1)}, s32[1,32]{1,0:T(1,128)}, u32[]{:S(2)}) copy-start(s32[1,32]{1,0:T(1,128)} %param.13) | copy-start | bytes 388
  12.8 9.4 %collective-permute-start = (bf16[3,128,2,128]{3,1,2,0:T(8,128)(2,1)}, bf16[3,128,2,128]{3,1,2,0:T(8,128)(2,1)}, u32[]{:S(2)}, u32[]{:S(2)}) collective-permute-start(bf16[3,128,2,128]{3,1,2,0:T(8,128)(2,1)} %bitcast.115), channel_id=1, source_target_pairs={{0,1},{1,0},{2,3},{3,2},{4,5},{5,4},{6,7},{7,6},{8,9},{9,8},{10,11... | collective-permute-start | bytes 589832 | tf_op jit(solution)/shard_map/ppermute | solution.py:29
  14.0 19.7 %collective-permute-start.1 = (bf16[3,128,2,128]{3,1,2,0:T(8,128)(2,1)}, bf16[3,128,2,128]{3,1,2,0:T(8,128)(2,1)S(1)}, u32[]{:S(2)}, u32[]{:S(2)}) collective-permute-start(bf16[3,128,2,128]{3,1,2,0:T(8,128)(2,1)} %bitcast.114), channel_id=1, source_target_pairs={{0,2},{1,3},{2,0},{3,1},{4,6},{5,7},{6,4},{7,5},{8,10},{9,11},{10,... | collective-permute-start | bytes 589832 | tf_op jit(solution)/shard_map/ppermute | solution.py:29
  16.6 27.3 %collective-permute-start.2 = (bf16[3,128,2,128]{3,1,2,0:T(8,128)(2,1)S(1)}, bf16[3,128,2,128]{3,1,2,0:T(8,128)(2,1)S(1)}, u32[]{:S(2)}, u32[]{:S(2)}) collective-permute-start(bf16[3,128,2,128]{3,1,2,0:T(8,128)(2,1)S(1)} %bitcast.134), channel_id=1, source_target_pairs={{0,3},{1,2},{2,1},{3,0},{4,7},{5,6},{6,5},{7,4},{8,11},{9,10},{10,... | collective-permute-start | bytes 589832 | tf_op jit(solution)/shard_map/ppermute | solution.py:29
  16.8 27.1 %collective-permute-start.3 = (bf16[3,128,2,128]{3,1,2,0:T(8,128)(2,1)S(1)}, bf16[3,128,2,128]{3,1,2,0:T(8,128)(2,1)S(1)}, u32[]{:S(2)}, u32[]{:S(2)}) collective-permute-start(bf16[3,128,2,128]{3,1,2,0:T(8,128)(2,1)S(1)} %bitcast.133), channel_id=1, source_target_pairs={{0,4},{1,5},{2,6},{3,7},{4,0},{5,1},{6,2},{7,3},{8,12},{9,13},{10,... | collective-permute-start | bytes 589832 | tf_op jit(solution)/shard_map/ppermute | solution.py:29
  19.6 28.8 %collective-permute-start.4 = (bf16[3,128,2,128]{3,1,2,0:T(8,128)(2,1)S(1)}, bf16[3,128,2,128]{3,1,2,0:T(8,128)(2,1)S(1)}, u32[]{:S(2)}, u32[]{:S(2)}) collective-permute-start(bf16[3,128,2,128]{3,1,2,0:T(8,128)(2,1)S(1)} %bitcast.132), channel_id=1, source_target_pairs={{0,5},{1,4},{2,7},{3,6},{4,1},{5,0},{6,3},{7,2},{8,13},{9,12},{10,... | collective-permute-start | bytes 589832 | tf_op jit(solution)/shard_map/ppermute | solution.py:29
  22.2 36.6 %collective-permute-start.5 = (bf16[3,128,2,128]{3,1,2,0:T(8,128)(2,1)S(1)}, bf16[3,128,2,128]{3,1,2,0:T(8,128)(2,1)S(1)}, u32[]{:S(2)}, u32[]{:S(2)}) collective-permute-start(bf16[3,128,2,128]{3,1,2,0:T(8,128)(2,1)S(1)} %bitcast.131), channel_id=1, source_target_pairs={{0,6},{1,7},{2,4},{3,5},{4,2},{5,3},{6,0},{7,1},{8,14},{9,15},{10,... | collective-permute-start | bytes 589832 | tf_op jit(solution)/shard_map/ppermute | solution.py:29
  33.6 32.0 %collective-permute-start.6 = (bf16[3,128,2,128]{3,1,2,0:T(8,128)(2,1)S(1)}, bf16[3,128,2,128]{3,1,2,0:T(8,128)(2,1)S(1)}, u32[]{:S(2)}, u32[]{:S(2)}) collective-permute-start(bf16[3,128,2,128]{3,1,2,0:T(8,128)(2,1)S(1)} %bitcast.130), channel_id=1, source_target_pairs={{0,7},{1,6},{2,5},{3,4},{4,3},{5,2},{6,1},{7,0},{8,15},{9,14},{10,... | collective-permute-start | bytes 589832 | tf_op jit(solution)/shard_map/ppermute | solution.py:29
  67.4 22.4 %copy-start = (bf16[256,2048]{1,0:T(8,128)(2,1)S(1)}, bf16[256,2048]{1,0:T(8,128)(2,1)}, u32[]{:S(2)}) copy-start(bf16[256,2048]{1,0:T(8,128)(2,1)} %param.11) | copy-start | bytes 3145732
  93.3 4.5 %copy-start.1 = (bf16[1024,256]{0,1:T(8,128)(2,1)}, bf16[1024,256]{0,1:T(8,128)(2,1)S(1)}, u32[]{:S(2)}) copy-start(bf16[1024,256]{0,1:T(8,128)(2,1)S(1)} %fusion.27) | copy-start | bytes 1572868
  93.3 4.8 %copy-start.3 = (bf16[1,1024,2048]{2,1,0:T(8,128)(2,1)S(1)}, bf16[1,1024,2048]{2,1,0:T(8,128)(2,1)}, u32[]{:S(2)}) copy-start(bf16[1,1024,2048]{2,1,0:T(8,128)(2,1)} %all-gather.6.cloned.1.call-done) | copy-start | bytes 12582916
  101.7 12.3 %copy-start.2 = (bf16[1024,256]{0,1:T(8,128)(2,1)S(1)}, bf16[1024,256]{0,1:T(8,128)(2,1)}, u32[]{:S(2)}) copy-start(bf16[1024,256]{0,1:T(8,128)(2,1)} %copy-done.1) | copy-start | bytes 1572868
  101.7 160.4 %all-gather.4.cloned.1.call-start = ((), (), s32[]{:S(2)}) async-start(), calls=%async_computation.2 | async-start | bytes 9437184 | tf_op jit(solution)/shard_map/all_gather | solution.py:92
  103.5 25.8 %all-to-all-start = ((bf16[1024,2,128]{2,1,0:T(2,128)(2,1)}), bf16[1024,2,128]{2,1,0:T(2,128)(2,1)S(1)}, u32[]{:S(2)}, u32[]{:S(2)}) async-start(bf16[1024,2,128]{2,1,0:T(2,128)(2,1)} %copy.122), calls=%async_computation | async-start | bytes 1048576 | tf_op jit(solution)/shard_map/all_to_all | solution.py:105
  129.3 52.1 %all-to-all-start.1 = ((bf16[3,1024,2,128]{3,2,0,1:T(2,128)(2,1)}), bf16[3,1024,2,128]{3,2,0,1:T(2,128)(2,1)S(1)}, u32[]{:S(2)}, u32[]{:S(2)}) async-start(bf16[3,1024,2,128]{3,2,0,1:T(2,128)(2,1)} %copy.133), calls=%async_computation.1 | async-start | bytes 3145728 | tf_op jit(solution)/shard_map/all_to_all | solution.py:119
Sparse Core Ops, SparseCore 0:
  9.6 80.1 all-gather.5
  101.8 76.4 all-reduce.1
  180.0 82.0 all-gather.3
